TPU v7x, 128 devices: a whole 4x4x4 slice. The times are simulated.
128 devices in a mesh: req: 8 (over z, core), shard: 16 (over x, y).
Axes of the slice: x: 4, y: 4, z: 4, core: 2. Of those that a mesh axis runs over, the one named last changes fastest.
Arguments:
- hidden_states: bfloat16 [16384, 1536], P(('req', 'shard')), may hold values from -6 to 6
- attn_gain: float32 [1536], replicated, may hold values from 0.5 to 1.5
- w_qkv: bfloat16 [1536, 2560], replicated, may hold values from -0.15625 to 0.15625
- w_out: bfloat16 [1536, 1536], replicated, may hold values from -0.15625 to 0.15625
- kv_cache: bfloat16 [8, 4096, 1024], P('req', 'shard'), may hold values from -80 to 80, as said below
- cached_len: int32 [8], P('req'), may hold values from 128 to 4096, as said below
- ffn_gain: float32 [1536], replicated, may hold values from 0.5 to 1.5
- w_router: bfloat16 [1536, 40], replicated, may hold values from -0.15625 to 0.15625
- expert_ids: int32 [16384, 8], P(('req', 'shard')), may hold values from 0 to 39, all different within a row; in each aligned block of 128 rows (0 to 127, 128 to 255, ...) at most 32 rows name the same one
- w_gate: bfloat16 [40, 512, 1536], P('req', 'shard'), may hold values from -0.15625 to 0.15625
- w_up: bfloat16 [40, 512, 1536], P('req', 'shard'), may hold values from -0.15625 to 0.15625
- w_down: bfloat16 [40, 512, 1536], P('req', 'shard'), may hold values from -0.25 to 0.25
Outputs:
- layer_out: bfloat16 [16384, 1536], P(('req', 'shard'))
Inputs may be any that keep to these rules, and one draw needn't show every extreme that they name: `cached_len`: each request's length is drawn either between 128 and 512 or between 3072 and 4096; some request has exactly 4096. `expert_ids`: among the 128 rows of one device no expert is named by more than 32 rows. `kv_cache`: cached keys and values, already rotated.
All inputs are finite; a program needn't handle non-finite values.
Results may differ from a plain program's by a relative error of at most 0.025.
Values may be sent and summed in bfloat16 or wider, within the bound.
No kernel may reach another device: no remote copies, remote signals or barrier semaphores. Data moves between devices by JAX's collectives and lax.ppermute only.
A program may use at most 192 MiB of HBM per device.

v0:
```python
import math

import jax
import jax.numpy as jnp
from jax import lax
from jax.sharding import PartitionSpec as P

D = 1536
HEADS = 24
KVH = 8
HD = 64
TOP = 8


EPSILON = 1e-05
NEG_FILL = -1e30
FAR_LIMIT = 1 << 30


def rms_scale(values, gain):
    floats = values.astype(jnp.float32)
    inverse = lax.rsqrt(jnp.mean(floats * floats, axis=-1, keepdims=True) + EPSILON)
    return (floats * inverse * gain).astype(jnp.bfloat16)


def rotate(values, positions):
    half_dim = values.shape[-1] // 2
    freqs = jnp.power(10000.0, -jnp.arange(half_dim, dtype=jnp.float32) / half_dim)
    angles = positions.astype(jnp.float32)[:, None] * freqs[None, :]
    cosine = jnp.cos(angles)[:, None, :]
    sine = jnp.sin(angles)[:, None, :]
    first = values[..., :half_dim]
    second = values[..., half_dim:]
    return jnp.concatenate(
        [first * cosine - second * sine, second * cosine + first * sine], axis=-1
    )


def empty_state(rows):
    groups = HEADS // KVH
    return (
        jnp.full((rows, KVH, groups), NEG_FILL, jnp.float32),
        jnp.zeros((rows, KVH, groups), jnp.float32),
        jnp.zeros((rows, KVH, groups, HD), jnp.float32),
    )


def attend_block(state, queries, query_pos, block, key_pos, key_limit):
    max_run, total, accum = state
    rows = block.shape[0]
    keys = block[:, : KVH * HD].reshape(rows, KVH, HD)
    values = block[:, KVH * HD :].reshape(rows, KVH, HD)
    scores = jnp.einsum(
        "tgqd,rgd->tgqr", queries, keys, preferred_element_type=jnp.float32
    ) * HD ** (-0.5)
    allowed = (key_pos[None, :] <= query_pos[:, None]) & (key_pos < key_limit)[None, :]
    allowed = allowed[:, None, None, :]
    block_max = jnp.max(jnp.where(allowed, scores, NEG_FILL), axis=-1)
    new_max = jnp.maximum(max_run, block_max)
    weights = jnp.where(allowed, jnp.exp(scores - new_max[..., None]), 0.0)
    factor = jnp.exp(max_run - new_max)
    total = total * factor + jnp.sum(weights, axis=-1)
    accum = accum * factor[..., None] + jnp.einsum(
        "tgqr,rgd->tgqd", weights.astype(jnp.bfloat16), values, preferred_element_type=jnp.float32
    )
    return (new_max, total, accum)


def fold_rows(state, queries, query_pos, piece, key_pos, key_limit):
    rows = piece.shape[0]
    step_rows = math.gcd(rows, 512)
    count = rows // step_rows
    blocks = piece.reshape(count, step_rows, piece.shape[1])
    positions = key_pos.reshape(count, step_rows)

    def advance(carry, item):
        return (attend_block(carry, queries, query_pos, item[0], item[1], key_limit), None)

    state, _ = lax.scan(advance, state, (blocks, positions))
    return state


def local(
    hidden_states,
    attn_gain,
    w_qkv,
    w_out,
    kv_cache,
    cached_len,
    ffn_gain,
    w_router,
    expert_ids,
    w_gate,
    w_up,
    w_down,
):
    groups = HEADS // KVH
    tok_rows = hidden_states.shape[0]
    shard_pos = lax.axis_index("shard")
    length = cached_len[0]
    normed = rms_scale(hidden_states, attn_gain)
    qkv = jnp.dot(normed, w_qkv, preferred_element_type=jnp.float32)
    positions = length + shard_pos * tok_rows + jnp.arange(tok_rows, dtype=jnp.int32)
    queries = rotate(qkv[:, : HEADS * HD].reshape(tok_rows, HEADS, HD), positions).astype(
        jnp.bfloat16
    )
    new_keys = rotate(
        qkv[:, HEADS * HD : (HEADS + KVH) * HD].reshape(tok_rows, KVH, HD), positions
    ).astype(jnp.bfloat16)
    new_values = qkv[:, (HEADS + KVH) * HD :].astype(jnp.bfloat16)
    new_kv = jnp.concatenate([new_keys.reshape(tok_rows, KVH * HD), new_values], axis=1)
    cache_local = kv_cache[0]
    query_heads = queries.reshape(tok_rows, KVH, groups, HD)
    piece = lax.all_gather(cache_local, "shard", axis=0, tiled=True)
    key_pos = jnp.arange(piece.shape[0], dtype=jnp.int32)
    state = fold_rows(empty_state(tok_rows), query_heads, positions, piece, key_pos, length)
    piece = lax.all_gather(new_kv, "shard", axis=0, tiled=True)
    key_pos = length + jnp.arange(piece.shape[0], dtype=jnp.int32)
    max_run, total, accum = fold_rows(state, query_heads, positions, piece, key_pos, FAR_LIMIT)
    attended = (accum / total[..., None]).astype(jnp.bfloat16)
    attended = attended.reshape(tok_rows, HEADS * HD)
    mid = (
        hidden_states.astype(jnp.float32)
        + jnp.dot(attended, w_out, preferred_element_type=jnp.float32)
    ).astype(jnp.bfloat16)
    normed2 = rms_scale(mid, ffn_gain)
    group_count = lax.axis_size("req")
    local_experts = w_gate.shape[0]
    expert_count = local_experts * group_count
    capacity = min(tok_rows, 5 * tok_rows * TOP // (4 * expert_count))
    logits = jnp.dot(normed2, w_router, preferred_element_type=jnp.float32)
    picked = expert_ids[:, :, None] == jnp.arange(expert_count, dtype=jnp.int32)[None, None, :]
    chosen = jnp.sum(jnp.where(picked, logits[:, None, :], 0.0), axis=-1)
    gates = jax.nn.softmax(chosen, axis=-1)
    flat_hot = picked.reshape(tok_rows * TOP, expert_count).astype(jnp.int32)
    ranks = jnp.cumsum(flat_hot, axis=0) - flat_hot
    slot_rank = jnp.sum(ranks * flat_hot, axis=-1)
    slots = expert_ids.reshape(-1) * capacity + slot_rank
    slot_table = (
        slots.reshape(tok_rows, TOP)[:, :, None]
        == jnp.arange(expert_count * capacity, dtype=jnp.int32)[None, None, :]
    )
    placing = jnp.any(slot_table, axis=1).astype(jnp.bfloat16)
    outgoing = jnp.einsum("ts,td->sd", placing, normed2, preferred_element_type=jnp.float32).astype(
        jnp.bfloat16
    )
    outgoing = outgoing.reshape(group_count, local_experts, capacity, D)
    arrived = lax.all_to_all(outgoing, "req", split_axis=0, concat_axis=0, tiled=True)
    gate_piece = lax.all_gather(w_gate, "shard", axis=1, tiled=True)
    up_piece = lax.all_gather(w_up, "shard", axis=1, tiled=True)
    down_piece = lax.all_gather(w_down, "shard", axis=1, tiled=True)
    gate = jnp.einsum("sjcd,jhd->sjch", arrived, gate_piece, preferred_element_type=jnp.float32)
    upper = jnp.einsum("sjcd,jhd->sjch", arrived, up_piece, preferred_element_type=jnp.float32)
    inner = (jax.nn.silu(gate) * upper).astype(jnp.bfloat16)
    summed = jnp.einsum("sjch,jhd->sjcd", inner, down_piece, preferred_element_type=jnp.float32)
    returned = lax.all_to_all(
        summed.astype(jnp.bfloat16), "req", split_axis=0, concat_axis=0, tiled=True
    )
    returned = returned.reshape(expert_count * capacity, D)
    expert_rows = returned[slots].reshape(tok_rows, TOP, D)
    mixture = jnp.sum(gates[:, :, None] * expert_rows.astype(jnp.float32), axis=1)
    return (mid.astype(jnp.float32) + mixture).astype(jnp.bfloat16)


def solution(mesh):
    return jax.shard_map(
        local,
        mesh=mesh,
        in_specs=(
            P(("req", "shard"), None),
            P(),
            P(),
            P(),
            P("req", "shard", None),
            P("req"),
            P(),
            P(),
            P(("req", "shard"), None),
            P("req", "shard", None),
            P("req", "shard", None),
            P("req", "shard", None),
        ),
        out_specs=P(("req", "shard"), None),
        check_vma=False,
    )
```

profile of v0, /device:TPU:30, one launch (start us, length us, event | category | flops | bytes accessed | tf_op | source)
XLA Modules:
  0.0 435.4 jit_solution(9446192712366749937)
XLA Ops:
  8.5 4.7 %fusion.66 = f32[128,2560]{1,0:T(8,128)S(1)} fusion(bf16[1536,2560]{1,0:T(8,128)(2,1)} %param.18, bf16[128,1536]{1,0:T(8,128)(2,1)} %param.16, f32[1536]{0:T(1024)} %param.17, f32[128]{0:T(128)S(1)} %add_rsqrt_fusion.1), kind=kOutput, calls=%fused_computation.80 | convolution fusion | flops 1007419392 | bytes 9574912 | tf_op jit(solution)/shard_map/dot_general | solution.py:102
  17.8 11.3 %reduce-window.6 = s32[40,8,128]{2,1,0:T(8,128)S(1)} reduce-window(s32[40,8,128]{2,1,0:T(8,128)S(1)} %fusion.73, s32[]{:T(128)} %copy.123), window={size=1x1x128 pad=0_0x0_0x127_0}, to_apply=%region_13.14 | reduce-window | flops 5201920 | bytes 327684 | tf_op jit(solution)/shard_map/reduce-window
  31.4 49.0 %all-gather.15.cloned.1.call-done = bf16[1,4096,1024]{2,1,0:T(8,128)(2,1)} async-done(((bf16[1,256,1024]{2,1,0:T(8,128)(2,1)}), bf16[1,4096,1024]{2,1,0:T(8,128)(2,1)}) %all-gather.15.cloned.1.call-update) | async-done | bytes 8388624 | tf_op jit(solution)/shard_map/all_gather | solution.py:114
  80.4 110.4 %while.31 = (s32[]{:T(128)}, f32[128,8,3]{0,2,1:T(4,128)S(1)}, f32[128,8,3]{0,2,1:T(4,128)S(1)}, f32[128,8,3,64]{0,3,2,1:T(8,128)}, s32[8,512]{1,0:T(8,128)S(1)}...) while((s32[]{:T(128)}, f32[128,8,3]{0,2,1:T(4,128)S(1)}, ...), condition=%wide.region_4.5_spmd.clone, body=%wide.region_1.4_spmd.clone.sunk | while | flops 420691584 | bytes 60104932 | solution.py:79
  83.2 3.8 fusion.130
  87.0 4.2 fusion.131
  96.8 3.8 fusion.130
  100.6 4.3 fusion.131
  110.5 3.8 fusion.130
  114.3 4.6 %fusion.131 = f32[128,8,3]{0,2,1:T(4,128)S(1)} fusion(f32[8,512,128,3]{2,1,3,0:T(8,128)} %get-tuple-element.405, f32[128,8,3]{0,2,1:T(4,128)S(1)} %select_maximum_fusion.2, pred[128,512]{0,1:T(8,128)(4,1)S(1)} %compare_and_fusion.5), kind=kLoop, calls=%fused_computation.29.clone.1 | loop fusion | flops 6288384 | bytes 6381568 | tf_op jit(solution)/shard_map/while/body/eval_jaxpr/reduce_sum | solution.py:62
  124.5 3.8 fusion.130
  128.3 4.3 fusion.131
  138.1 3.8 fusion.130
  141.9 4.2 fusion.131
  151.7 3.8 fusion.130
  155.5 4.4 %fusion.131 = f32[128,8,3]{0,2,1:T(4,128)S(1)} fusion(f32[8,512,128,3]{2,1,3,0:T(8,128)} %get-tuple-element.405, f32[128,8,3]{0,2,1:T(4,128)S(1)} %select_maximum_fusion.2, pred[128,512]{0,1:T(8,128)(4,1)S(1)} %compare_and_fusion.5), kind=kLoop, calls=%fused_computation.29.clone.1 | loop fusion | flops 6288384 | bytes 6381568 | tf_op jit(solution)/shard_map/while/body/eval_jaxpr/reduce_sum | solution.py:62
  165.4 3.8 fusion.130
  169.3 4.9 %fusion.131 = f32[128,8,3]{0,2,1:T(4,128)S(1)} fusion(f32[8,512,128,3]{2,1,3,0:T(8,128)} %get-tuple-element.405, f32[128,8,3]{0,2,1:T(4,128)S(1)} %select_maximum_fusion.2, pred[128,512]{0,1:T(8,128)(4,1)S(1)} %compare_and_fusion.5), kind=kLoop, calls=%fused_computation.29.clone.1 | loop fusion | flops 6288384 | bytes 6381568 | tf_op jit(solution)/shard_map/while/body/eval_jaxpr/reduce_sum | solution.py:62
  179.7 3.8 fusion.130
  183.5 4.3 fusion.131
  190.8 28.0 %while.30 = (s32[]{:T(128)}, f32[128,8,3]{0,2,1:T(4,128)S(1)}, f32[128,8,3]{0,2,1:T(4,128)S(1)}, f32[128,8,3,64]{0,3,2,1:T(8,128)}, s32[4,512]{1,0:T(4,128)S(1)}...) while((s32[]{:T(128)}, f32[128,8,3]{0,2,1:T(4,128)S(1)}, ...), condition=%wide.region_8.9_spmd.clone, body=%wide.region_5.8_spmd.clone.sunk | while | flops 420485760 | bytes 34939048 | solution.py:79
  220.0 3.3 multiply_reduce_fusion
  226.5 4.5 %all-to-all-start = ((bf16[8,5,32,1536]{3,2,1,0:T(8,128)(2,1)}), bf16[8,5,32,1536]{3,2,1,0:T(8,128)(2,1)}, u32[]{:S(2)}, u32[]{:S(2)}) async-start(bf16[8,5,32,1536]{3,2,1,0:T(8,128)(2,1)} %bitcast.216), calls=%async_computation | async-start | bytes 7864320 | tf_op jit(solution)/shard_map/all_to_all | solution.py:148
  231.0 46.8 %all-to-all-done = bf16[8,5,32,1536]{3,2,1,0:T(8,128)(2,1)} async-done(((bf16[8,5,32,1536]{3,2,1,0:T(8,128)(2,1)}), bf16[8,5,32,1536]{3,2,1,0:T(8,128)(2,1)}, u32[]{:S(2)}, u32[]{:S(2)}) %all-to-all-start) | async-done | bytes 3932192 | tf_op jit(solution)/shard_map/all_to_all | solution.py:148
  277.9 8.1 %fusion.41 = f32[5,8,32,512]{3,2,1,0:T(8,128)} fusion(bf16[5,512,1536]{2,1,0:T(8,128)(2,1)} %all-gather.9.cloned.1.call-done, bf16[8,5,32,1536]{3,2,1,0:T(8,128)(2,1)} %all-to-all-done), kind=kOutput, calls=%fused_computation.50 | convolution fusion | flops 2013265920 | bytes 14417920 | tf_op jit(solution)/shard_map/sjcd,jhd->sjch/dot_general | solution.py:152
  286.0 58.0 %all-gather.11.cloned.1.call-done = bf16[5,512,1536]{2,1,0:T(8,128)(2,1)} async-done(((bf16[5,32,1536]{2,1,0:T(8,128)(2,1)}), bf16[5,512,1536]{2,1,0:T(8,128)(2,1)}) %all-gather.11.cloned.1.call-update) | async-done | bytes 7864336 | tf_op jit(solution)/shard_map/all_gather | solution.py:150
  344.0 13.5 %fusion.48 = bf16[8,5,32,1536]{3,2,0,1:T(8,128)(2,1)} fusion(bf16[5,512,1536]{2,1,0:T(8,128)(2,1)} %all-gather.13.cloned.1.call-done, f32[5,8,32,512]{3,2,1,0:T(8,128)} %fusion.41, bf16[5,512,1536]{2,1,0:T(8,128)(2,1)} %all-gather.11.cloned.1.call-done, bf16[8,5,32,1536]{3,2,1,0:T(8,128)(2,1)} %all-to-all-done), kind=kOutput, calls=%fused_computation.58 | convolution fusion | flops 4032430080 | bytes 26214400 | tf_op jit(solution)/shard_map/sjch,jhd->sjcd/dot_general | solution.py:155
  357.5 4.5 %copy.70 = bf16[8,5,32,1536]{3,2,1,0:T(8,128)(2,1)} copy(bf16[8,5,32,1536]{3,2,0,1:T(8,128)(2,1)} %fusion.48) | data formatting | bytes 7864320 | tf_op jit(solution)/shard_map/convert_element_type | solution.py:157
  362.1 4.7 %all-to-all-start.1 = ((bf16[8,5,32,1536]{3,2,1,0:T(8,128)(2,1)}), bf16[8,5,32,1536]{3,2,1,0:T(8,128)(2,1)}, u32[]{:S(2)}, u32[]{:S(2)}) async-start(bf16[8,5,32,1536]{3,2,1,0:T(8,128)(2,1)} %copy.70), calls=%async_computation.1 | async-start | bytes 7864320 | tf_op jit(solution)/shard_map/all_to_all | solution.py:156
  367.5 46.0 %all-to-all-done.1 = bf16[8,5,32,1536]{3,2,1,0:T(8,128)(2,1)} async-done(((bf16[8,5,32,1536]{3,2,1,0:T(8,128)(2,1)}), bf16[8,5,32,1536]{3,2,1,0:T(8,128)(2,1)}, u32[]{:S(2)}, u32[]{:S(2)}) %all-to-all-start.1) | async-done | bytes 3932192 | tf_op jit(solution)/shard_map/all_to_all | solution.py:156
  413.4 9.9 %gather_fusion = bf16[1024,1536]{1,0:T(8,128)(2,1)} fusion(bf16[1280,1536]{1,0:T(8,128)(2,1)} %bitcast.21, s32[1024]{0:T(1024)S(1)} %broadcast_clamp_fusion), kind=kCustom, calls=%fused_computation | custom fusion | bytes 6295552 | tf_op jit(solution)/shard_map/gather | solution.py:160
  423.3 4.7 %fusion.43 = f32[128,1536]{1,0:T(8,128)S(1)} fusion(bf16[1024,1536]{1,0:T(8,128)(2,1)} %gather_fusion, f32[128,8]{1,0:T(8,128)S(1)} %copy.62), kind=kLoop, calls=%fused_computation.54 | loop fusion | flops 4521984 | bytes 3936256 | tf_op jit(solution)/shard_map/reduce_sum | solution.py:161
  (261 shorter events, 85.8 us)
Async XLA Ops:
  6.5 360.4 %copy-start = (bf16[1536,40]{0,1:T(8,128)(2,1)S(1)}, bf16[1536,40]{0,1:T(8,128)(2,1)}, u32[]{:S(2)}) copy-start(bf16[1536,40]{0,1:T(8,128)(2,1)} %param.23) | copy-start | bytes 368644
  6.5 73.9 %all-gather.15.cloned.1.call-start = ((), (), s32[]{:S(2)}) async-start(), calls=%async_computation.6 | async-start | bytes 8912896 | tf_op jit(solution)/shard_map/all_gather | solution.py:114
  7.3 183.5 %all-gather.7.cloned.1.call-start = ((), (), s32[]{:S(2)}) async-start(), calls=%async_computation.2 | async-start | bytes 4456448 | tf_op jit(solution)/shard_map/all_gather | solution.py:117
  8.5 8.7 %copy-start.8 = (s32[128,8]{0,1:T(8,128)S(1)}, s32[128,8]{0,1:T(8,128)}, u32[]{:S(2)}) copy-start(s32[128,8]{0,1:T(8,128)} %param.24) | copy-start | bytes 12292
  15.1 215.9 %all-gather.9.cloned.1.call-start = ((), (), s32[]{:S(2)}) async-start(), calls=%async_computation.3 | async-start | bytes 8355840 | tf_op jit(solution)/shard_map/all_gather | solution.py:149
  15.9 270.1 %all-gather.13.cloned.1.call-start = ((), (), s32[]{:S(2)}) async-start(), calls=%async_computation.5 | async-start | bytes 8355840 | tf_op jit(solution)/shard_map/all_gather | solution.py:151
  16.4 327.5 %all-gather.11.cloned.1.call-start = ((), (), s32[]{:S(2)}) async-start(), calls=%async_computation.4 | async-start | bytes 8355840 | tf_op jit(solution)/shard_map/all_gather | solution.py:150
  83.2 8.1 %copy-start.3 = (f32[128,8,3,64]{0,3,2,1:T(8,128)S(1)}, f32[128,8,3,64]{0,3,2,1:T(8,128)}, u32[]{:S(2)}) copy-start(f32[128,8,3,64]{0,3,2,1:T(8,128)} %get-tuple-element.423) | copy-start | bytes 2359300 | tf_op jit(solution)/shard_map/while
  87.0 4.6 %copy-start.1 = (f32[8,512,128,3]{2,1,3,0:T(8,128)S(1)}, f32[8,512,128,3]{2,1,3,0:T(8,128)}, u32[]{:S(2)}) copy-start(f32[8,512,128,3]{2,1,3,0:T(8,128)} %get-tuple-element.405) | copy-start | bytes 18874372 | tf_op jit(solution)/shard_map/while
  96.8 8.2 %copy-start.3 = (f32[128,8,3,64]{0,3,2,1:T(8,128)S(1)}, f32[128,8,3,64]{0,3,2,1:T(8,128)}, u32[]{:S(2)}) copy-start(f32[128,8,3,64]{0,3,2,1:T(8,128)} %get-tuple-element.423) | copy-start | bytes 2359300 | tf_op jit(solution)/shard_map/while
  100.6 4.7 %copy-start.1 = (f32[8,512,128,3]{2,1,3,0:T(8,128)S(1)}, f32[8,512,128,3]{2,1,3,0:T(8,128)}, u32[]{:S(2)}) copy-start(f32[8,512,128,3]{2,1,3,0:T(8,128)} %get-tuple-element.405) | copy-start | bytes 18874372 | tf_op jit(solution)/shard_map/while
  106.8 0.9 copy-start.4
  110.5 8.4 %copy-start.3 = (f32[128,8,3,64]{0,3,2,1:T(8,128)S(1)}, f32[128,8,3,64]{0,3,2,1:T(8,128)}, u32[]{:S(2)}) copy-start(f32[128,8,3,64]{0,3,2,1:T(8,128)} %get-tuple-element.423) | copy-start | bytes 2359300 | tf_op jit(solution)/shard_map/while
  114.3 5.0 %copy-start.1 = (f32[8,512,128,3]{2,1,3,0:T(8,128)S(1)}, f32[8,512,128,3]{2,1,3,0:T(8,128)}, u32[]{:S(2)}) copy-start(f32[8,512,128,3]{2,1,3,0:T(8,128)} %get-tuple-element.405) | copy-start | bytes 18874372 | tf_op jit(solution)/shard_map/while
  124.4 8.2 %copy-start.3 = (f32[128,8,3,64]{0,3,2,1:T(8,128)S(1)}, f32[128,8,3,64]{0,3,2,1:T(8,128)}, u32[]{:S(2)}) copy-start(f32[128,8,3,64]{0,3,2,1:T(8,128)} %get-tuple-element.423) | copy-start | bytes 2359300 | tf_op jit(solution)/shard_map/while
  128.2 4.7 %copy-start.1 = (f32[8,512,128,3]{2,1,3,0:T(8,128)S(1)}, f32[8,512,128,3]{2,1,3,0:T(8,128)}, u32[]{:S(2)}) copy-start(f32[8,512,128,3]{2,1,3,0:T(8,128)} %get-tuple-element.405) | copy-start | bytes 18874372 | tf_op jit(solution)/shard_map/while
  138.1 8.1 %copy-start.3 = (f32[128,8,3,64]{0,3,2,1:T(8,128)S(1)}, f32[128,8,3,64]{0,3,2,1:T(8,128)}, u32[]{:S(2)}) copy-start(f32[128,8,3,64]{0,3,2,1:T(8,128)} %get-tuple-element.423) | copy-start | bytes 2359300 | tf_op jit(solution)/shard_map/while
  141.9 4.6 %copy-start.1 = (f32[8,512,128,3]{2,1,3,0:T(8,128)S(1)}, f32[8,512,128,3]{2,1,3,0:T(8,128)}, u32[]{:S(2)}) copy-start(f32[8,512,128,3]{2,1,3,0:T(8,128)} %get-tuple-element.405) | copy-start | bytes 18874372 | tf_op jit(solution)/shard_map/while
  151.7 8.2 %copy-start.3 = (f32[128,8,3,64]{0,3,2,1:T(8,128)S(1)}, f32[128,8,3,64]{0,3,2,1:T(8,128)}, u32[]{:S(2)}) copy-start(f32[128,8,3,64]{0,3,2,1:T(8,128)} %get-tuple-element.423) | copy-start | bytes 2359300 | tf_op jit(solution)/shard_map/while
  155.5 4.8 %copy-start.1 = (f32[8,512,128,3]{2,1,3,0:T(8,128)S(1)}, f32[8,512,128,3]{2,1,3,0:T(8,128)}, u32[]{:S(2)}) copy-start(f32[8,512,128,3]{2,1,3,0:T(8,128)} %get-tuple-element.405) | copy-start | bytes 18874372 | tf_op jit(solution)/shard_map/while
  165.4 8.8 %copy-start.3 = (f32[128,8,3,64]{0,3,2,1:T(8,128)S(1)}, f32[128,8,3,64]{0,3,2,1:T(8,128)}, u32[]{:S(2)}) copy-start(f32[128,8,3,64]{0,3,2,1:T(8,128)} %get-tuple-element.423) | copy-start | bytes 2359300 | tf_op jit(solution)/shard_map/while
  169.2 5.3 %copy-start.1 = (f32[8,512,128,3]{2,1,3,0:T(8,128)S(1)}, f32[8,512,128,3]{2,1,3,0:T(8,128)}, u32[]{:S(2)}) copy-start(f32[8,512,128,3]{2,1,3,0:T(8,128)} %get-tuple-element.405) | copy-start | bytes 18874372 | tf_op jit(solution)/shard_map/while
  179.7 8.2 %copy-start.3 = (f32[128,8,3,64]{0,3,2,1:T(8,128)S(1)}, f32[128,8,3,64]{0,3,2,1:T(8,128)}, u32[]{:S(2)}) copy-start(f32[128,8,3,64]{0,3,2,1:T(8,128)} %get-tuple-element.423) | copy-start | bytes 2359300 | tf_op jit(solution)/shard_map/while
  183.5 4.9 %copy-start.1 = (f32[8,512,128,3]{2,1,3,0:T(8,128)S(1)}, f32[8,512,128,3]{2,1,3,0:T(8,128)}, u32[]{:S(2)}) copy-start(f32[8,512,128,3]{2,1,3,0:T(8,128)} %get-tuple-element.405) | copy-start | bytes 18874372 | tf_op jit(solution)/shard_map/while
  190.8 29.3 %copy-start.2 = (bf16[128,1536]{1,0:T(8,128)(2,1)S(1)}, bf16[128,1536]{1,0:T(8,128)(2,1)}, u32[]{:S(2)}) copy-start(bf16[128,1536]{1,0:T(8,128)(2,1)} %param.16) | copy-start | bytes 1179652
  193.0 2.5 copy-start.5
  200.0 2.5 copy-start.5
  207.0 2.5 copy-start.5
  214.0 2.5 copy-start.5
  218.8 4.5 %copy-start.7 = (f32[1536]{0:T(1024)S(1)}, f32[1536]{0:T(1024)}, u32[]{:S(2)}) copy-start(f32[1536]{0:T(1024)} %param.22) | copy-start | bytes 18436
  226.5 51.4 %all-to-all-start = ((bf16[8,5,32,1536]{3,2,1,0:T(8,128)(2,1)}), bf16[8,5,32,1536]{3,2,1,0:T(8,128)(2,1)}, u32[]{:S(2)}, u32[]{:S(2)}) async-start(bf16[8,5,32,1536]{3,2,1,0:T(8,128)(2,1)} %bitcast.216), calls=%async_computation | async-start | bytes 7864320 | tf_op jit(solution)/shard_map/all_to_all | solution.py:148
  362.1 51.4 %all-to-all-start.1 = ((bf16[8,5,32,1536]{3,2,1,0:T(8,128)(2,1)}), bf16[8,5,32,1536]{3,2,1,0:T(8,128)(2,1)}, u32[]{:S(2)}, u32[]{:S(2)}) async-start(bf16[8,5,32,1536]{3,2,1,0:T(8,128)(2,1)} %copy.70), calls=%async_computation.1 | async-start | bytes 7864320 | tf_op jit(solution)/shard_map/all_to_all | solution.py:156
  (11 other events, 9.9 us)
Sparse Core Ops, SparseCore 0:
  9.5 70.8 all-gather.14
  82.5 50.9 all-gather.6
  135.7 68.0 all-gather.8
  205.8 68.0 all-gather.12
  275.9 68.0 all-gather.10
where the time goes:
time: 439 us; the launch traced here: 435 us
  waiting for transfers between devices  202 us (46%)
  matrix products  85.3 us (19%)
  other arithmetic  71.1 us (16%)
  local copies, waits for them, and re-layouts  52.4 us (12%)
  between operations  14.1 us (3%)
  starting transfers between devices  9.4 us (2%)
    all_gather x1, waiting for transfers between devices, local(): up_piece = lax.all_gather(w_up, 'shard', axis=1, tiled=True)  58 us
    all_gather x1, waiting for transfers between devices, local(): piece = lax.all_gather(cache_local, 'shard', axis=0, tiled=True)  49 us
    all_to_all x1, waiting for transfers between devices, local(): lax.all_to_all(outgoing, 'req', split_axis=0, concat_axis=0, tiled=True)  46.8 us
    all_to_all x1, waiting for transfers between devices, local(): lax.all_to_all(summed.astype(jnp.bfloat16), 'req', split_axis=0, concat_a...  46 us
    reduce_sum x12, other arithmetic, attend_block(): total = total * factor + jnp.sum(weights, axis=-1)  40.5 us
    dot_general x12, matrix products, attend_block(): jnp.einsum('tgqd,rgd->tgqr', queries, keys, preferred_element_type=jnp.fl...  34.7 us
    dynamic_slice x24, local copies, waits for them, and re-layouts, fold_rows(): state, _ = lax.scan(advance, state, (blocks, positions))  22.2 us
    dot_general x12, matrix products, attend_block(): jnp.einsum('tgqr,rgd->tgqd', weights.astype(jnp.bfloat16), values, prefer...  17.5 us
  transfers between devices with their start and end apart: 7, of which 4 were waited for; matrix products, arithmetic and copies ran while one was open for 37% of the time, Pallas kernels for 0%

commit v1 on v0

--- a/solution.py
+++ b/solution.py
@@ -146,9 +146,11 @@
     )
     outgoing = outgoing.reshape(group_count, local_experts, capacity, D)
     arrived = lax.all_to_all(outgoing, "req", split_axis=0, concat_axis=0, tiled=True)
-    gate_piece = lax.all_gather(w_gate, "shard", axis=1, tiled=True)
-    up_piece = lax.all_gather(w_up, "shard", axis=1, tiled=True)
-    down_piece = lax.all_gather(w_down, "shard", axis=1, tiled=True)
+    weights = jnp.concatenate([w_gate, w_up, w_down], axis=-1)
+    weights = lax.all_gather(weights, "shard", axis=1, tiled=True)
+    gate_piece = weights[..., :D]
+    up_piece = weights[..., D : 2 * D]
+    down_piece = weights[..., 2 * D :]
     gate = jnp.einsum("sjcd,jhd->sjch", arrived, gate_piece, preferred_element_type=jnp.float32)
     upper = jnp.einsum("sjcd,jhd->sjch", arrived, up_piece, preferred_element_type=jnp.float32)
     inner = (jax.nn.silu(gate) * upper).astype(jnp.bfloat16)

time: 439 us -> 384 us (0.87)
  blocking collectives: 0 us -> 51.2 us
  waiting for transfers between devices: 202 us -> 151 us
  matrix products: 85.3 us -> 60.4 us
  other arithmetic: 71.1 us -> 48.2 us
  starting transfers between devices: 9.4 us -> 4.59 us
    all_to_all x0 -> x1, blocking collectives: none -> 51.2 us  [local(): lax.all_to_all(outgoing, 'req', split_axis=0, concat_axis=0, tiled=True)]
    all_to_all x1 -> x0, waiting for transfers between devices: 46.8 us -> none  [local(): lax.all_to_all(outgoing, 'req', split_axis=0, concat_axis=0, tiled=True)]
    reduce_sum x12, other arithmetic: 40.5 us -> 15.3 us  [attend_block(): total = total * factor + jnp.sum(weights, axis=-1)]
    dot_general x12, matrix products: 34.7 us -> 13 us  [attend_block(): jnp.einsum('tgqd,rgd->tgqr', queries, keys, preferred_element_type=jnp.fl...]
    all_to_all x1 -> x0, starting transfers between devices: 4.51 us -> none  [local(): lax.all_to_all(outgoing, 'req', split_axis=0, concat_axis=0, tiled=True)]
    all_gather x3 -> x1, waiting for transfers between devices: 58 us -> 55.3 us  [local(): weights = lax.all_gather(weights, 'shard', axis=1, tiled=True)]
    while x76 -> x60, local copies, waits for them, and re-layouts: 13.4 us -> 10.8 us
  transfers between devices with their start and end apart: 7 -> 4, of which waited for: 4 -> 3; matrix products, arithmetic and copies ran while one was open for 37% -> 28% of each run, Pallas kernels for 0% -> 0%
where the time goes in v1:
time: 384 us; the launch traced here: 380 us
  waiting for transfers between devices  151 us (39%)
  matrix products  60.4 us (16%)
  blocking collectives  51.2 us (13%)
  local copies, waits for them, and re-layouts  49.8 us (13%)
  other arithmetic  48.2 us (13%)
  between operations  14.1 us (4%)
  starting transfers between devices  4.59 us (1%)
    all_gather x1, waiting for transfers between devices, local(): weights = lax.all_gather(weights, 'shard', axis=1, tiled=True)  55.3 us
    all_to_all x1, blocking collectives, local(): lax.all_to_all(outgoing, 'req', split_axis=0, concat_axis=0, tiled=True)  51.2 us
    all_gather x1, waiting for transfers between devices, local(): piece = lax.all_gather(cache_local, 'shard', axis=0, tiled=True)  48.3 us
    all_to_all x1, waiting for transfers between devices, local(): lax.all_to_all(summed.astype(jnp.bfloat16), 'req', split_axis=0, concat_a...  46.2 us
    dynamic_slice x24, local copies, waits for them, and re-layouts, fold_rows(): state, _ = lax.scan(advance, state, (blocks, positions))  22.3 us
    dot_general x12, matrix products, attend_block(): jnp.einsum('tgqr,rgd->tgqd', weights.astype(jnp.bfloat16), values, prefer...  17.3 us
    reduce_sum x12, other arithmetic, attend_block(): total = total * factor + jnp.sum(weights, axis=-1)  15.3 us
    dot_general x12, matrix products, attend_block(): jnp.einsum('tgqd,rgd->tgqr', queries, keys, preferred_element_type=jnp.fl...  13 us
  transfers between devices with their start and end apart: 4, of which 3 were waited for; matrix products, arithmetic and copies ran while one was open for 28% of the time, Pallas kernels for 0%

profile of v1, /device:TPU:30, one launch (start us, length us, event | category | flops | bytes accessed | tf_op | source)
XLA Modules:
  0.0 379.8 jit_solution(826455171912664360)
XLA Ops:
  8.5 4.7 %fusion.60 = f32[128,2560]{1,0:T(8,128)S(1)} fusion(bf16[1536,2560]{1,0:T(8,128)(2,1)} %param.18, bf16[128,1536]{1,0:T(8,128)(2,1)} %param.16, f32[1536]{0:T(1024)} %param.17, f32[128]{0:T(128)S(1)} %add_rsqrt_fusion.1), kind=kOutput, calls=%fused_computation.82 | convolution fusion | flops 1007419392 | bytes 9574912 | tf_op jit(solution)/shard_map/dot_general | solution.py:102
  15.3 2.3 pad_maximum_fusion
  18.0 11.3 %reduce-window.6 = s32[40,8,128]{2,1,0:T(8,128)S(1)} reduce-window(s32[40,8,128]{2,1,0:T(8,128)S(1)} %fusion.67, s32[]{:T(128)} %copy.121), window={size=1x1x128 pad=0_0x0_0x127_0}, to_apply=%region_13.14 | reduce-window | flops 5201920 | bytes 327684 | tf_op jit(solution)/shard_map/reduce-window
  30.3 1.6 fusion.41
  32.0 48.3 %all-gather.9.cloned.1.call-done = bf16[1,4096,1024]{2,1,0:T(8,128)(2,1)} async-done(((bf16[1,256,1024]{2,1,0:T(8,128)(2,1)}), bf16[1,4096,1024]{2,1,0:T(8,128)(2,1)}) %all-gather.9.cloned.1.call-update) | async-done | bytes 8388624 | tf_op jit(solution)/shard_map/all_gather | solution.py:114
  80.3 60.8 %while.31 = (s32[]{:T(128)}, f32[128,8,3]{0,2,1:T(4,128)S(1)}, f32[128,8,3]{0,2,1:T(4,128)S(1)}, f32[128,8,3,64]{0,3,2,1:T(8,128)}, s32[8,512]{1,0:T(8,128)S(1)}...) while((s32[]{:T(128)}, f32[128,8,3]{0,2,1:T(4,128)S(1)}, ...), condition=%wide.region_4.5_spmd.clone, body=%wide.region_1.4_spmd.clone.sunk | while | flops 420691584 | bytes 34939080 | solution.py:79
  85.6 1.4 fusion.119
  93.2 1.4 fusion.119
  100.8 1.4 fusion.119
  108.3 1.4 fusion.119
  115.9 1.4 fusion.119
  123.5 1.4 fusion.119
  126.8 1.3 constant_dynamic-slice_fusion.9
  131.2 1.4 fusion.119
  138.8 1.4 fusion.119
  141.1 27.9 %while.30 = (s32[]{:T(128)}, f32[128,8,3]{0,2,1:T(4,128)S(1)}, f32[128,8,3]{0,2,1:T(4,128)S(1)}, f32[128,8,3,64]{0,3,2,1:T(8,128)}, s32[4,512]{1,0:T(4,128)S(1)}...) while((s32[]{:T(128)}, f32[128,8,3]{0,2,1:T(4,128)S(1)}, ...), condition=%wide.region_8.9_spmd.clone, body=%wide.region_5.8_spmd.clone.sunk | while | flops 420485760 | bytes 34939048 | solution.py:79
  145.7 1.4 fusion.110
  148.3 1.4 constant_dynamic-slice_fusion.8
  152.8 1.4 fusion.110
  155.4 1.3 constant_dynamic-slice_fusion.8
  159.8 1.4 fusion.110
  166.7 1.4 fusion.110
  170.3 3.2 multiply_reduce_fusion
  174.8 51.2 %all_to_all.10 = bf16[8,5,32,1536]{3,2,1,0:T(8,128)(2,1)} all-to-all(bf16[8,5,32,1536]{3,2,1,0:T(8,128)(2,1)S(1)} %bitcast.209), channel_id=1, replica_groups=mesh['req'=8,'shard'=16] {'req'}, dimensions={0} | all-to-all | bytes 7864320 | tf_op jit(solution)/shard_map/all_to_all | solution.py:148
  226.0 55.3 %all-gather.7.cloned.1.call-done = bf16[5,512,4608]{2,1,0:T(8,128)(2,1)} async-done(((bf16[5,32,4608]{2,1,0:T(8,128)(2,1)}), bf16[5,512,4608]{2,1,0:T(8,128)(2,1)}) %all-gather.7.cloned.1.call-update) | async-done | bytes 23592976 | tf_op jit(solution)/shard_map/all_gather | solution.py:150
  281.3 8.1 %fusion.38 = f32[5,512,8,32]{1,3,2,0:T(8,128)} fusion(bf16[5,512,4608]{2,1,0:T(8,128)(2,1)} %all-gather.7.cloned.1.call-done, bf16[8,5,32,1536]{3,2,1,0:T(8,128)(2,1)} %all_to_all.10), kind=kOutput, calls=%fused_computation.49 | convolution fusion | flops 2013265920 | bytes 14417920 | tf_op jit(solution)/shard_map/sjcd,jhd->sjch/dot_general | solution.py:154
  289.4 12.6 %fusion.43 = bf16[8,5,32,1536]{3,2,0,1:T(8,128)(2,1)} fusion(bf16[5,512,4608]{2,1,0:T(8,128)(2,1)} %all-gather.7.cloned.1.call-done, f32[5,512,8,32]{1,3,2,0:T(8,128)} %fusion.38, bf16[8,5,32,1536]{3,2,1,0:T(8,128)(2,1)} %all_to_all.10), kind=kOutput, calls=%fused_computation.58 | convolution fusion | flops 4032430080 | bytes 26214400 | tf_op jit(solution)/shard_map/sjch,jhd->sjcd/dot_general | solution.py:157
  302.0 4.5 %copy.70 = bf16[8,5,32,1536]{3,2,1,0:T(8,128)(2,1)} copy(bf16[8,5,32,1536]{3,2,0,1:T(8,128)(2,1)} %fusion.43) | data formatting | bytes 7864320 | tf_op jit(solution)/shard_map/convert_element_type | solution.py:159
  306.4 4.5 %all-to-all-start.1 = ((bf16[8,5,32,1536]{3,2,1,0:T(8,128)(2,1)}), bf16[8,5,32,1536]{3,2,1,0:T(8,128)(2,1)}, u32[]{:S(2)}, u32[]{:S(2)}) async-start(bf16[8,5,32,1536]{3,2,1,0:T(8,128)(2,1)} %copy.70), calls=%async_computation.1 | async-start | bytes 7864320 | tf_op jit(solution)/shard_map/all_to_all | solution.py:158
  311.6 46.2 %all-to-all-done.1 = bf16[8,5,32,1536]{3,2,1,0:T(8,128)(2,1)} async-done(((bf16[8,5,32,1536]{3,2,1,0:T(8,128)(2,1)}), bf16[8,5,32,1536]{3,2,1,0:T(8,128)(2,1)}, u32[]{:S(2)}, u32[]{:S(2)}) %all-to-all-start.1) | async-done | bytes 3932192 | tf_op jit(solution)/shard_map/all_to_all | solution.py:158
  357.8 9.9 %gather_fusion = bf16[1024,1536]{1,0:T(8,128)(2,1)} fusion(bf16[1280,1536]{1,0:T(8,128)(2,1)} %bitcast.21, s32[1024]{0:T(1024)S(1)} %broadcast_clamp_fusion), kind=kCustom, calls=%fused_computation | custom fusion | bytes 6295552 | tf_op jit(solution)/shard_map/gather | solution.py:162
  367.7 4.7 %fusion.40 = f32[128,1536]{1,0:T(8,128)S(1)} fusion(bf16[1024,1536]{1,0:T(8,128)(2,1)} %gather_fusion, f32[128,8]{1,0:T(8,128)S(1)} %copy.62), kind=kLoop, calls=%fused_computation.54 | loop fusion | flops 4521984 | bytes 3936256 | tf_op jit(solution)/shard_map/reduce_sum | solution.py:163
  (243 shorter events, 75.0 us)
Async XLA Ops:
  6.5 304.5 %copy-start = (bf16[1536,40]{0,1:T(8,128)(2,1)S(1)}, bf16[1536,40]{0,1:T(8,128)(2,1)}, u32[]{:S(2)}) copy-start(bf16[1536,40]{0,1:T(8,128)(2,1)} %param.23) | copy-start | bytes 368644
  6.5 73.8 %all-gather.9.cloned.1.call-start = ((), (), s32[]{:S(2)}) async-start(), calls=%async_computation.4 | async-start | bytes 8912896 | tf_op jit(solution)/shard_map/all_gather | solution.py:114
  7.3 133.9 %all-gather.5.cloned.1.call-start = ((), (), s32[]{:S(2)}) async-start(), calls=%async_computation.2 | async-start | bytes 4456448 | tf_op jit(solution)/shard_map/all_gather | solution.py:117
  8.5 6.8 %copy-start.6 = (bf16[5,32,1536]{2,1,0:T(8,128)(2,1)S(1)}, bf16[5,32,1536]{2,1,0:T(8,128)(2,1)}, u32[]{:S(2)}) copy-start(bf16[5,32,1536]{2,1,0:T(8,128)(2,1)} %param.27) | copy-start | bytes 1474564
  8.5 6.8 %copy-start.7 = (bf16[5,32,1536]{2,1,0:T(8,128)(2,1)S(1)}, bf16[5,32,1536]{2,1,0:T(8,128)(2,1)}, u32[]{:S(2)}) copy-start(bf16[5,32,1536]{2,1,0:T(8,128)(2,1)} %param.26) | copy-start | bytes 1474564
  13.2 4.4 %copy-start.9 = (s32[128,8]{0,1:T(8,128)S(1)}, s32[128,8]{0,1:T(8,128)}, u32[]{:S(2)}) copy-start(s32[128,8]{0,1:T(8,128)} %param.24) | copy-start | bytes 12292
  15.2 266.1 %all-gather.7.cloned.1.call-start = ((), (), s32[]{:S(2)}) async-start(), calls=%async_computation.3 | async-start | bytes 25067520 | tf_op jit(solution)/shard_map/all_gather | solution.py:150
  83.1 2.4 copy-start.2
  87.0 0.9 copy-start.3
  90.7 2.4 copy-start.2
  94.6 0.9 copy-start.3
  98.3 2.4 copy-start.2
  102.2 0.9 copy-start.3
  105.9 2.4 copy-start.2
  109.8 0.9 copy-start.3
  113.5 2.4 copy-start.2
  117.4 0.9 copy-start.3
  121.1 2.4 copy-start.2
  125.0 0.9 copy-start.3
  128.7 2.4 copy-start.2
  132.6 0.9 copy-start.3
  136.3 2.4 copy-start.2
  140.2 0.9 copy-start.3
  141.1 29.2 %copy-start.1 = (bf16[128,1536]{1,0:T(8,128)(2,1)S(1)}, bf16[128,1536]{1,0:T(8,128)(2,1)}, u32[]{:S(2)}) copy-start(bf16[128,1536]{1,0:T(8,128)(2,1)} %param.16) | copy-start | bytes 1179652
  143.3 2.4 copy-start.4
  147.2 0.9 copy-start.5
  150.3 2.4 copy-start.4
  157.3 2.4 copy-start.4
  161.2 0.9 copy-start.5
  164.3 2.4 copy-start.4
  169.0 4.5 %copy-start.8 = (f32[1536]{0:T(1024)S(1)}, f32[1536]{0:T(1024)}, u32[]{:S(2)}) copy-start(f32[1536]{0:T(1024)} %param.22) | copy-start | bytes 18436
  306.4 51.4 %all-to-all-start.1 = ((bf16[8,5,32,1536]{3,2,1,0:T(8,128)(2,1)}), bf16[8,5,32,1536]{3,2,1,0:T(8,128)(2,1)}, u32[]{:S(2)}, u32[]{:S(2)}) async-start(bf16[8,5,32,1536]{3,2,1,0:T(8,128)(2,1)} %copy.70), calls=%async_computation.1 | async-start | bytes 7864320 | tf_op jit(solution)/shard_map/all_to_all | solution.py:158
  (2 other events, 1.8 us)
Sparse Core Ops, SparseCore 0:
  9.5 70.8 all-gather.8
  82.5 51.0 all-gather.4
  135.7 145.6 all-gather.6

commit v2 on v1

--- a/solution.py
+++ b/solution.py
@@ -1,8 +1,11 @@
+import functools
 import math
 
 import jax
 import jax.numpy as jnp
 from jax import lax
+from jax.experimental import pallas as pl
+from jax.experimental.pallas import tpu as pltpu
 from jax.sharding import PartitionSpec as P
 
 D = 1536
@@ -15,6 +18,78 @@
 EPSILON = 1e-05
 NEG_FILL = -1e30
 FAR_LIMIT = 1 << 30
+BLK = 512
+NEG = NEG_FILL
+
+def attn_kernel(meta_ref, q_ref, cache_ref, new_ref, o_ref, m_sc, l_sc, acc_sc, *, n_cache, rows):
+    i = pl.program_id(0)
+    length = meta_ref[0]
+    qbase = meta_ref[1]
+
+    @pl.when(i == 0)
+    def _():
+        m_sc[...] = jnp.full(m_sc.shape, NEG, jnp.float32)
+        l_sc[...] = jnp.zeros(l_sc.shape, jnp.float32)
+        acc_sc[...] = jnp.zeros(acc_sc.shape, jnp.float32)
+
+    def step(kv_ref, allowed):
+        for g in range(KVH):
+            q = q_ref[g]
+            k = kv_ref[:, g * HD:(g + 1) * HD]
+            v = kv_ref[:, KVH * HD + g * HD:KVH * HD + (g + 1) * HD]
+            s = lax.dot_general(q, k, (((1,), (1,)), ((), ())), preferred_element_type=jnp.float32) * (HD ** -0.5)
+            s = jnp.where(allowed, s, NEG)
+            m_prev = m_sc[g]
+            m_new = jnp.maximum(m_prev, jnp.max(s, axis=-1, keepdims=True))
+            p = jnp.where(allowed, jnp.exp(s - m_new), 0.0)
+            factor = jnp.exp(m_prev - m_new)
+            l_sc[g] = l_sc[g] * factor + jnp.sum(p, axis=-1, keepdims=True)
+            acc_sc[g] = acc_sc[g] * factor + jnp.dot(p.astype(jnp.bfloat16), v, preferred_element_type=jnp.float32)
+            m_sc[g] = m_new
+
+    @pl.when((i < n_cache) & (i * BLK < length))
+    def _():
+        key = i * BLK + lax.broadcasted_iota(jnp.int32, (rows, BLK), 1)
+        step(cache_ref, key < length)
+
+    j = i - n_cache
+    @pl.when((i >= n_cache) & (j * BLK <= qbase + (rows // (HEADS // KVH)) - 1))
+    def _():
+        key = j * BLK + lax.broadcasted_iota(jnp.int32, (rows, BLK), 1)
+        qpos = qbase + lax.broadcasted_iota(jnp.int32, (rows, BLK), 0) % (rows // (HEADS // KVH))
+        step(new_ref, key <= qpos)
+
+    @pl.when(i == pl.num_programs(0) - 1)
+    def _():
+        for g in range(KVH):
+            o_ref[g] = (acc_sc[g] / l_sc[g]).astype(o_ref.dtype)
+
+def attention(queries, cache, new_kv, length, qbase):
+    rows = queries.shape[1]
+    n_cache = cache.shape[0] // BLK
+    n_new = new_kv.shape[0] // BLK
+    meta = jnp.stack([length, qbase]).astype(jnp.int32)
+    kern = functools.partial(attn_kernel, n_cache=n_cache, rows=rows)
+    return pl.pallas_call(
+        kern,
+        out_shape=jax.ShapeDtypeStruct((KVH, rows, HD), jnp.bfloat16),
+        grid_spec=pltpu.PrefetchScalarGridSpec(
+            num_scalar_prefetch=1,
+            grid=(n_cache + n_new,),
+            in_specs=[
+                pl.BlockSpec((KVH, rows, HD), lambda i, m: (0, 0, 0)),
+                pl.BlockSpec((BLK, 2 * KVH * HD), lambda i, m: (jnp.minimum(i, n_cache - 1), 0)),
+                pl.BlockSpec((BLK, 2 * KVH * HD), lambda i, m: (jnp.maximum(i - n_cache, 0), 0)),
+            ],
+            out_specs=pl.BlockSpec((KVH, rows, HD), lambda i, m: (0, 0, 0)),
+            scratch_shapes=[
+                pltpu.VMEM((KVH, rows, 1), jnp.float32),
+                pltpu.VMEM((KVH, rows, 1), jnp.float32),
+                pltpu.VMEM((KVH, rows, HD), jnp.float32),
+            ],
+        ),
+        compiler_params=pltpu.CompilerParams(dimension_semantics=("arbitrary",)),
+    )(meta, queries, cache, new_kv)
 
 
 def rms_scale(values, gain):
@@ -34,50 +109,6 @@
     return jnp.concatenate(
         [first * cosine - second * sine, second * cosine + first * sine], axis=-1
     )
-
-
-def empty_state(rows):
-    groups = HEADS // KVH
-    return (
-        jnp.full((rows, KVH, groups), NEG_FILL, jnp.float32),
-        jnp.zeros((rows, KVH, groups), jnp.float32),
-        jnp.zeros((rows, KVH, groups, HD), jnp.float32),
-    )
-
-
-def attend_block(state, queries, query_pos, block, key_pos, key_limit):
-    max_run, total, accum = state
-    rows = block.shape[0]
-    keys = block[:, : KVH * HD].reshape(rows, KVH, HD)
-    values = block[:, KVH * HD :].reshape(rows, KVH, HD)
-    scores = jnp.einsum(
-        "tgqd,rgd->tgqr", queries, keys, preferred_element_type=jnp.float32
-    ) * HD ** (-0.5)
-    allowed = (key_pos[None, :] <= query_pos[:, None]) & (key_pos < key_limit)[None, :]
-    allowed = allowed[:, None, None, :]
-    block_max = jnp.max(jnp.where(allowed, scores, NEG_FILL), axis=-1)
-    new_max = jnp.maximum(max_run, block_max)
-    weights = jnp.where(allowed, jnp.exp(scores - new_max[..., None]), 0.0)
-    factor = jnp.exp(max_run - new_max)
-    total = total * factor + jnp.sum(weights, axis=-1)
-    accum = accum * factor[..., None] + jnp.einsum(
-        "tgqr,rgd->tgqd", weights.astype(jnp.bfloat16), values, preferred_element_type=jnp.float32
-    )
-    return (new_max, total, accum)
-
-
-def fold_rows(state, queries, query_pos, piece, key_pos, key_limit):
-    rows = piece.shape[0]
-    step_rows = math.gcd(rows, 512)
-    count = rows // step_rows
-    blocks = piece.reshape(count, step_rows, piece.shape[1])
-    positions = key_pos.reshape(count, step_rows)
-
-    def advance(carry, item):
-        return (attend_block(carry, queries, query_pos, item[0], item[1], key_limit), None)
-
-    state, _ = lax.scan(advance, state, (blocks, positions))
-    return state
 
 
 def local(
@@ -109,15 +140,12 @@
     ).astype(jnp.bfloat16)
     new_values = qkv[:, (HEADS + KVH) * HD :].astype(jnp.bfloat16)
     new_kv = jnp.concatenate([new_keys.reshape(tok_rows, KVH * HD), new_values], axis=1)
-    cache_local = kv_cache[0]
-    query_heads = queries.reshape(tok_rows, KVH, groups, HD)
-    piece = lax.all_gather(cache_local, "shard", axis=0, tiled=True)
-    key_pos = jnp.arange(piece.shape[0], dtype=jnp.int32)
-    state = fold_rows(empty_state(tok_rows), query_heads, positions, piece, key_pos, length)
-    piece = lax.all_gather(new_kv, "shard", axis=0, tiled=True)
-    key_pos = length + jnp.arange(piece.shape[0], dtype=jnp.int32)
-    max_run, total, accum = fold_rows(state, query_heads, positions, piece, key_pos, FAR_LIMIT)
-    attended = (accum / total[..., None]).astype(jnp.bfloat16)
+    cache = lax.all_gather(kv_cache[0], "shard", axis=0, tiled=True)
+    fresh = lax.all_gather(new_kv, "shard", axis=0, tiled=True)
+    query_rows = queries.reshape(tok_rows, KVH, groups, HD).transpose(1, 2, 0, 3)
+    query_rows = query_rows.reshape(KVH, groups * tok_rows, HD)
+    attended = attention(query_rows, cache, fresh, length, shard_pos * tok_rows)
+    attended = attended.reshape(KVH, groups, tok_rows, HD).transpose(2, 0, 1, 3)
     attended = attended.reshape(tok_rows, HEADS * HD)
     mid = (
         hidden_states.astype(jnp.float32)

time: 384 us -> 388 us (1.010)
  Pallas kernels: 0 us -> 41.2 us
  blocking collectives: 51.2 us -> 91.5 us
  local copies, waits for them, and re-layouts: 49.8 us -> 18.1 us
  matrix products: 60.4 us -> 30.1 us
  other arithmetic: 48.2 us -> 25.3 us
  waiting for transfers between devices: 151 us -> 160 us
    all_gather x2, waiting for transfers between devices: 48.4 us -> 104 us  [the longest x1 72.5 us: local(): cache = lax.all_gather(kv_cache[0], 'shard', axis=0, tiled=True)]
    all_gather x1, waiting for transfers between devices: 55.3 us -> 9.12 us  [local(): weights = lax.all_gather(weights, 'shard', axis=1, tiled=True)]
    pallas_call x0 -> x1, Pallas kernels: none -> 41.2 us  [attention(): pl.pallas_call(kern, out_shape=jax.ShapeDtypeStruct((KVH, rows, HD), jnp....]
    all_to_all x1, blocking collectives: 51.2 us -> 91.5 us  [local(): lax.all_to_all(outgoing, 'req', split_axis=0, concat_axis=0, tiled=True)]
    dot_general x24 -> x0, matrix products: 30.3 us -> none  [the longest x12 17.3 us: attend_block(): jnp.einsum('tgqr,rgd->tgqd', weights.astype(jnp.bfloat16), values, prefer...]
    dynamic_slice x24 -> x0, local copies, waits for them, and re-layouts: 22.3 us -> none  [fold_rows(): state, _ = lax.scan(advance, state, (blocks, positions))]
    reduce_sum x12 -> x0, other arithmetic: 15.3 us -> none  [attend_block(): total = total * factor + jnp.sum(weights, axis=-1)]
    while x60 -> x0, local copies, waits for them, and re-layouts: 10.8 us -> none
  transfers between devices with their start and end apart: 4 -> 4, of which waited for: 3 -> 4; matrix products, arithmetic and copies ran while one was open for 28% -> 7% of each run, Pallas kernels for 0% -> 11%
where the time goes in v2:
time: 388 us; the launch traced here: 385 us
  waiting for transfers between devices  160 us (41%)
  blocking collectives  91.5 us (24%)
  Pallas kernels  41.2 us (11%)
  matrix products  30.1 us (8%)
  other arithmetic  25.3 us (7%)
  local copies, waits for them, and re-layouts  18.1 us (5%)
  between operations  14.1 us (4%)
  starting transfers between devices  4.59 us (1%)
    all_to_all x1, blocking collectives, local(): lax.all_to_all(outgoing, 'req', split_axis=0, concat_axis=0, tiled=True)  91.5 us
    all_gather x1, waiting for transfers between devices, local(): cache = lax.all_gather(kv_cache[0], 'shard', axis=0, tiled=True)  72.5 us
    all_to_all x1, waiting for transfers between devices, local(): lax.all_to_all(summed.astype(jnp.bfloat16), 'req', split_axis=0, concat_a...  46.2 us
    pallas_call x1, Pallas kernels, attention(): pl.pallas_call(kern, out_shape=jax.ShapeDtypeStruct((KVH, rows, HD), jnp....  41.2 us
    all_gather x1, waiting for transfers between devices, local(): fresh = lax.all_gather(new_kv, 'shard', axis=0, tiled=True)  31.4 us
    dot_general x1, matrix products, local(): jnp.einsum('sjch,jhd->sjcd', inner, down_piece, preferred_element_type=jn...  12.6 us
    another operation x5, other arithmetic  11.6 us
    gather x1, local copies, waits for them, and re-layouts, local(): expert_rows = returned[slots].reshape(tok_rows, TOP, D)  9.89 us
  transfers between devices with their start and end apart: 4, of which 4 were waited for; matrix products, arithmetic and copies ran while one was open for 7% of the time, Pallas kernels for 11%

profile of v2, /device:TPU:30, one launch (start us, length us, event | category | flops | bytes accessed | tf_op | source)
XLA Modules:
  0.0 384.9 jit_solution(15682190046234132992)
XLA Ops:
  6.6 1.2 fusion.20
  7.8 4.7 %fusion.23 = f32[128,2560]{1,0:T(8,128)S(1)} fusion(bf16[1536,2560]{1,0:T(8,128)(2,1)} %param.14, bf16[128,1536]{1,0:T(8,128)(2,1)} %param.12, f32[1536]{0:T(1024)} %param.13, f32[128]{0:T(128)S(1)} %add_rsqrt_fusion.1), kind=kOutput, calls=%fused_computation.37 | convolution fusion | flops 1007419392 | bytes 9574912 | tf_op jit(solution)/shard_map/dot_general | solution.py:133
  13.3 0.1 copy.53
  13.4 0.1 multiply_cosine_fusion
  13.7 0.7 pad_maximum_fusion.2
  14.5 0.7 all-gather.9.cloned.1.call-update
  15.3 2.3 pad_maximum_fusion
  18.0 11.3 %reduce-window.6 = s32[40,8,128]{2,1,0:T(8,128)S(1)} reduce-window(s32[40,8,128]{2,1,0:T(8,128)S(1)} %fusion.30, s32[]{:T(128)} %constant.34.clone.1), window={size=1x1x128 pad=0_0x0_0x127_0}, to_apply=%region_5.6 | reduce-window | flops 5201920 | bytes 327684 | tf_op jit(solution)/shard_map/reduce-window
  29.4 0.1 copy.60
  29.9 0.3 copy.50
  30.2 0.4 copy.52
  30.6 0.4 copy.51
  31.0 0.7 pad_add_fusion.meta_ref
  31.7 1.3 pad_maximum_fusion.1
  33.1 1.6 fusion.4
  34.7 31.4 %all-gather.5.cloned.1.call-done.new_ref = bf16[2048,1024]{1,0:T(8,128)(2,1)} async-done(((bf16[128,1024]{1,0:T(8,128)(2,1)}), bf16[2048,1024]{1,0:T(8,128)(2,1)}) %all-gather.5.cloned.1.call-update) | async-done | bytes 4194320 | tf_op jit(solution)/shard_map/all_gather | solution.py:144
  66.1 72.5 %all-gather.9.cloned.1.call-done = bf16[1,4096,1024]{2,1,0:T(8,128)(2,1)} async-done(((bf16[1,256,1024]{2,1,0:T(8,128)(2,1)}), bf16[1,4096,1024]{2,1,0:T(8,128)(2,1)}) %all-gather.9.cloned.1.call-update) | async-done | bytes 8388624 | tf_op jit(solution)/shard_map/all_gather | solution.py:143
  138.6 41.2 %shard_map.118 = bf16[8,384,64]{2,1,0:T(8,128)(2,1)} custom-call(s32[2]{0:T(128)} %pad_add_fusion.meta_ref, bf16[8,384,64]{2,1,0:T(8,128)(2,1)} %bitcast.95, bf16[4096,1024]{1,0:T(8,128)(2,1)} %bitcast.93, bf16[2048,1024]{1,0:T(8,128)(2,1)} %all-gather.5.cloned.1.call-done.new_ref), custom_call_target="tpu_custom_call" | custom-call | tf_op jit(solution)/shard_map/pallas_call | solution.py:73
  179.9 1.4 copy.55
  181.3 3.2 multiply_reduce_fusion
  184.6 1.3 convolution_convert_fusion
  185.8 91.5 %all_to_all.10 = bf16[8,5,32,1536]{3,2,1,0:T(8,128)(2,1)} all-to-all(bf16[8,5,32,1536]{3,2,1,0:T(8,128)(2,1)S(1)} %bitcast.92), channel_id=1, replica_groups=mesh['req'=8,'shard'=16] {'req'}, dimensions={0} | all-to-all | bytes 7864320 | tf_op jit(solution)/shard_map/all_to_all | solution.py:176
  277.3 9.1 %all-gather.7.cloned.1.call-done = bf16[5,512,4608]{2,1,0:T(8,128)(2,1)} async-done(((bf16[5,32,4608]{2,1,0:T(8,128)(2,1)}), bf16[5,512,4608]{2,1,0:T(8,128)(2,1)}) %all-gather.7.cloned.1.call-update) | async-done | bytes 23592976 | tf_op jit(solution)/shard_map/all_gather | solution.py:178
  286.4 8.1 %fusion.1 = f32[5,512,8,32]{1,3,2,0:T(8,128)} fusion(bf16[5,512,4608]{2,1,0:T(8,128)(2,1)} %all-gather.7.cloned.1.call-done, bf16[8,5,32,1536]{3,2,1,0:T(8,128)(2,1)} %all_to_all.10), kind=kOutput, calls=%fused_computation.4 | convolution fusion | flops 2013265920 | bytes 14417920 | tf_op jit(solution)/shard_map/sjcd,jhd->sjch/dot_general | solution.py:182
  294.5 12.6 %fusion.6 = bf16[8,5,32,1536]{3,2,0,1:T(8,128)(2,1)} fusion(bf16[5,512,4608]{2,1,0:T(8,128)(2,1)} %all-gather.7.cloned.1.call-done, f32[5,512,8,32]{1,3,2,0:T(8,128)} %fusion.1, bf16[8,5,32,1536]{3,2,1,0:T(8,128)(2,1)} %all_to_all.10), kind=kOutput, calls=%fused_computation.13 | convolution fusion | flops 4032430080 | bytes 26214400 | tf_op jit(solution)/shard_map/sjch,jhd->sjcd/dot_general | solution.py:185
  307.1 4.5 %copy.64 = bf16[8,5,32,1536]{3,2,1,0:T(8,128)(2,1)} copy(bf16[8,5,32,1536]{3,2,0,1:T(8,128)(2,1)} %fusion.6) | data formatting | bytes 7864320 | tf_op jit(solution)/shard_map/convert_element_type | solution.py:187
  311.5 4.5 %all-to-all-start.1 = ((bf16[8,5,32,1536]{3,2,1,0:T(8,128)(2,1)}), bf16[8,5,32,1536]{3,2,1,0:T(8,128)(2,1)}, u32[]{:S(2)}, u32[]{:S(2)}) async-start(bf16[8,5,32,1536]{3,2,1,0:T(8,128)(2,1)} %copy.64), calls=%async_computation.1 | async-start | bytes 7864320 | tf_op jit(solution)/shard_map/all_to_all | solution.py:186
  316.2 0.3 fusion.35
  316.7 46.2 %all-to-all-done.1 = bf16[8,5,32,1536]{3,2,1,0:T(8,128)(2,1)} async-done(((bf16[8,5,32,1536]{3,2,1,0:T(8,128)(2,1)}), bf16[8,5,32,1536]{3,2,1,0:T(8,128)(2,1)}, u32[]{:S(2)}, u32[]{:S(2)}) %all-to-all-start.1) | async-done | bytes 3932192 | tf_op jit(solution)/shard_map/all_to_all | solution.py:186
  362.9 9.9 %gather_fusion = bf16[1024,1536]{1,0:T(8,128)(2,1)} fusion(bf16[1280,1536]{1,0:T(8,128)(2,1)} %bitcast.25, s32[1024]{0:T(1024)S(1)} %broadcast_clamp_fusion), kind=kCustom, calls=%fused_computation | custom fusion | bytes 6295552 | tf_op jit(solution)/shard_map/gather | solution.py:190
  372.8 4.7 %fusion.3 = f32[128,1536]{1,0:T(8,128)S(1)} fusion(bf16[1024,1536]{1,0:T(8,128)(2,1)} %gather_fusion, f32[128,8]{1,0:T(8,128)S(1)} %copy.56), kind=kLoop, calls=%fused_computation.9 | loop fusion | flops 4521984 | bytes 3936256 | tf_op jit(solution)/shard_map/reduce_sum | solution.py:191
  377.5 0.9 add_convert_fusion
  (48 shorter events, 1.6 us)
Async XLA Ops:
  6.5 309.6 %copy-start = (bf16[1536,40]{0,1:T(8,128)(2,1)S(1)}, bf16[1536,40]{0,1:T(8,128)(2,1)}, u32[]{:S(2)}) copy-start(bf16[1536,40]{0,1:T(8,128)(2,1)} %param.19) | copy-start | bytes 368644
  6.5 59.5 %all-gather.5.cloned.1.call-start = ((), (), s32[]{:S(2)}) async-start(), calls=%async_computation.2 | async-start | bytes 4456448 | tf_op jit(solution)/shard_map/all_gather | solution.py:144
  12.4 2.9 copy-start.2
  12.4 2.9 copy-start.3
  12.5 5.1 %copy-start.5 = (s32[128,8]{0,1:T(8,128)S(1)}, s32[128,8]{0,1:T(8,128)}, u32[]{:S(2)}) copy-start(s32[128,8]{0,1:T(8,128)} %param.20) | copy-start | bytes 12292
  14.5 124.1 %all-gather.9.cloned.1.call-start = ((), (), s32[]{:S(2)}) async-start(), calls=%async_computation.4 | async-start | bytes 8912896 | tf_op jit(solution)/shard_map/all_gather | solution.py:143
  15.2 271.2 %all-gather.7.cloned.1.call-start = ((), (), s32[]{:S(2)}) async-start(), calls=%async_computation.3 | async-start | bytes 25067520 | tf_op jit(solution)/shard_map/all_gather | solution.py:178
  138.6 42.7 %copy-start.1 = (bf16[128,1536]{1,0:T(8,128)(2,1)S(1)}, bf16[128,1536]{1,0:T(8,128)(2,1)}, u32[]{:S(2)}) copy-start(bf16[128,1536]{1,0:T(8,128)(2,1)} %param.12) | copy-start | bytes 1179652
  179.9 4.7 %copy-start.4 = (f32[1536]{0:T(1024)S(1)}, f32[1536]{0:T(1024)}, u32[]{:S(2)}) copy-start(f32[1536]{0:T(1024)} %param.18) | copy-start | bytes 18436
  311.5 51.4 %all-to-all-start.1 = ((bf16[8,5,32,1536]{3,2,1,0:T(8,128)(2,1)}), bf16[8,5,32,1536]{3,2,1,0:T(8,128)(2,1)}, u32[]{:S(2)}, u32[]{:S(2)}) async-start(bf16[8,5,32,1536]{3,2,1,0:T(8,128)(2,1)} %copy.64), calls=%async_computation.1 | async-start | bytes 7864320 | tf_op jit(solution)/shard_map/all_to_all | solution.py:186
Sparse Core Ops, SparseCore 0:
  14.6 51.4 all-gather.4
  68.2 70.3 all-gather.8
  140.8 145.6 all-gather.6
